TPU v7x, 256 devices: a whole 4x4x8 slice. The times are simulated.
256 devices in a mesh: row: 16 (over z, y_lo), col: 16 (over y_hi, x, core).
Axes of the slice: x: 4, y: 4 (y_hi: 2, y_lo: 2; y = y_hi * 2 + y_lo), z: 8, core: 2. Of those that a mesh axis runs over, the one named last changes fastest.
Arguments:
- points: float32 [32, 65536], P(None, ('row', 'col')), may hold values from -6 to 6
- candidates: float32 [32, 16384], P(None, ('row', 'col')), may hold values from -6 to 6
- length_scales: float32 [32], replicated, may hold values from 1.5 to 4
- signal_var: float32 [1], replicated, may hold values from 0.5 to 2
- noise_var: float32 [1], replicated, may hold values from 0.1 to 1
- cand_prior: float32 [16384], P(('row', 'col')), may hold values from -6 to 6
- weights: float32 [16, 65536], P(None, ('row', 'col')), may hold values from -6 to 6
- residual: float32 [16, 65536], P(None, ('row', 'col')), may hold values from -300 to 300, as said below
- direction: float32 [16, 65536], P(None, ('row', 'col')), may hold values from -300 to 300, as said below
Outputs:
- weights_new: float32 [16, 65536], P(None, ('row', 'col'))
- residual_new: float32 [16, 65536], P(None, ('row', 'col'))
- direction_new: float32 [16, 65536], P(None, ('row', 'col'))
- cand_fit: float32 [16, 16384], P(None, ('row', 'col'))
Inputs may be any that keep to these rules, and one draw needn't show every extreme that they name: `residual`: real values. `direction`: real values.
All inputs are finite; a program needn't handle non-finite values.
Results may differ from a plain program's by a relative error of at most 0.011.
Values may be sent and summed in bfloat16 or wider, within the bound.
No kernel may reach another device: no remote copies, remote signals or barrier semaphores. Data moves between devices by JAX's collectives and lax.ppermute only.
A program may use at most 64 MiB of HBM per device.

v0:
```python
import math
import jax
import jax.numpy as jnp
from jax import lax
from jax.sharding import PartitionSpec as P

root_five = math.sqrt(5.0)
contract_first = (((0,), (0,)), ((), ()))
contract_last = (((1,), (1,)), ((), ()))


def square_norms(scaled):
    return jnp.sum(jnp.square(scaled.astype(jnp.float32)), axis=0)


def matern_block(row_pts, row_sq, col_pts, col_sq, signal_scalar):
    inner_prod = lax.dot_general(
        row_pts, col_pts, contract_first, preferred_element_type=jnp.float32
    )
    dist_sq = jnp.maximum(row_sq[:, None] + col_sq[None, :] - 2.0 * inner_prod, 0.0)
    distance = jnp.sqrt(dist_sq)
    kern_vals = (
        signal_scalar
        * (1.0 + root_five * distance + 5.0 / 3.0 * dist_sq)
        * jnp.exp(-root_five * distance)
    )
    return kern_vals.astype(jnp.bfloat16)


def kernel_apply(running, row_pts, row_sq, col_pts, col_sq, vectors, signal_scalar):
    row_count = row_pts.shape[1]
    width_all = col_pts.shape[1]
    block_len = math.gcd(width_all, max(256, 1048576 // row_count))
    num_blocks = width_all // block_len

    def one_block(total, pieces):
        pts_blk, sq_blk, vec_blk = pieces
        kern_vals = matern_block(row_pts, row_sq, pts_blk, sq_blk, signal_scalar)
        return (
            total
            + lax.dot_general(
                vec_blk, kern_vals, contract_last, preferred_element_type=jnp.float32
            ),
            None,
        )

    feature_count = col_pts.shape[0]
    pts_blocks = col_pts.reshape(feature_count, num_blocks, block_len).transpose(1, 0, 2)
    sq_blocks = col_sq.reshape(num_blocks, block_len)
    vec_blocks = vectors.reshape(vectors.shape[0], num_blocks, block_len).transpose(1, 0, 2)
    result, ignored = lax.scan(one_block, running, (pts_blocks, sq_blocks, vec_blocks))
    return result


def per_device(
    points,
    candidates,
    length_scales,
    signal_var,
    noise_var,
    cand_prior,
    weights,
    residual,
    direction,
):
    scaled = (points / length_scales[:, None]).astype(jnp.bfloat16)
    cand_scaled = (candidates / length_scales[:, None]).astype(jnp.bfloat16)
    signal_scalar = signal_var[0]
    dir_low = direction.astype(jnp.bfloat16)
    col_total = direction.shape[0]
    norm_now = lax.psum(jnp.sum(residual * residual, axis=1), ("row", "col"))
    row_pts, row_cands = (
        lax.all_gather(scaled, "col", axis=1, tiled=True),
        lax.all_gather(cand_scaled, "col", axis=1, tiled=True),
    )
    col_pts = lax.all_gather(scaled, "row", axis=1, tiled=True)
    row_sq = square_norms(row_pts)
    col_sq = square_norms(col_pts)
    cand_sq = square_norms(row_cands)
    start_rows = jnp.zeros((col_total, row_pts.shape[1]), jnp.float32)
    pts_piece = col_pts
    sq_piece = col_sq
    partial_rows = kernel_apply(
        start_rows,
        row_pts,
        row_sq,
        pts_piece,
        sq_piece,
        lax.all_gather(dir_low, "row", axis=1, tiled=True),
        signal_scalar,
    )
    kernel_out = lax.psum_scatter(partial_rows, "col", scatter_dimension=1, tiled=True)
    image_vec = kernel_out + noise_var[0] * direction
    curvature = lax.psum(jnp.sum(direction * image_vec, axis=1), ("row", "col"))
    step_len = norm_now / curvature
    weights_new = weights + step_len[:, None] * direction
    residual_new = residual - step_len[:, None] * image_vec
    norm_next = lax.psum(jnp.sum(residual_new * residual_new, axis=1), ("row", "col"))
    direction_new = residual_new + (norm_next / norm_now)[:, None] * direction
    w_low = weights_new.astype(jnp.bfloat16)
    start_cands = jnp.zeros((col_total, row_cands.shape[1]), jnp.float32)
    pts_piece = col_pts
    sq_piece = col_sq
    partial_fit = kernel_apply(
        start_cands,
        row_cands,
        cand_sq,
        pts_piece,
        sq_piece,
        lax.all_gather(w_low, "row", axis=1, tiled=True),
        signal_scalar,
    )
    fitted = lax.psum_scatter(partial_fit, "col", scatter_dimension=1, tiled=True)
    cand_fit = cand_prior[None, :] + fitted
    return (weights_new, residual_new, direction_new, cand_fit)


def solution(mesh):
    placed = (
        P(None, ("row", "col")),
        P(None, ("row", "col")),
        P(),
        P(),
        P(),
        P(("row", "col")),
        P(None, ("row", "col")),
        P(None, ("row", "col")),
        P(None, ("row", "col")),
    )
    return jax.shard_map(
        per_device,
        mesh=mesh,
        in_specs=placed,
        out_specs=(
            P(None, ("row", "col")),
            P(None, ("row", "col")),
            P(None, ("row", "col")),
            P(None, ("row", "col")),
        ),
        check_vma=False,
    )
```

profile of v0, /device:TPU:2, one launch (start us, length us, event | category | flops | bytes accessed | tf_op | source)
XLA Modules:
  0.0 508.7 jit_solution(10705769252974074291)
XLA Ops:
  8.1 37.8 %all_gather.17 = bf16[32,4096]{1,0:T(8,128)(2,1)S(1)} all-gather(bf16[32,256]{1,0:T(8,128)(2,1)S(1)} %divide_convert_fusion), channel_id=1, replica_groups=mesh['row'=16,'col'=16] {'row'}, dimensions={1}, use_global_device_ids=true | all-gather | bytes 278528 | tf_op jit(solution)/shard_map/all_gather | solution.py:76
  45.9 20.4 %all_gather.16 = bf16[32,4096]{1,0:T(8,128)(2,1)S(1)} all-gather(bf16[32,256]{1,0:T(8,128)(2,1)S(1)} %divide_convert_fusion), channel_id=1, replica_groups=mesh['row'=16,'col'=16] {'col'}, dimensions={1}, use_global_device_ids=true | all-gather | bytes 278528 | tf_op jit(solution)/shard_map/all_gather | solution.py:73
  67.0 30.2 %all_gather.15 = bf16[16,4096]{1,0:T(8,128)(2,1)S(1)} all-gather(bf16[16,256]{1,0:T(8,128)(2,1)S(1)} %convert_element_type.27), channel_id=1, replica_groups=mesh['row'=16,'col'=16] {'row'}, dimensions={1}, use_global_device_ids=true | all-gather | bytes 139264 | tf_op jit(solution)/shard_map/all_gather | solution.py:89
  97.2 62.3 %while.22 = (s32[]{:T(128)}, f32[16,4096]{1,0:T(8,128)S(1)}, bf16[16,16,256]{2,1,0:T(8,128)(2,1)S(1)}, f32[]{:T(128)}, f32[4096]{0:T(1024)S(1)}, /*index=5*/f32[...) while((s32[]{:T(128)}, f32[16,4096]{1,0:T(8,128)S(1)}, ...), condition=%wide.region_5.6_spmd.clone, body=%wide.region_4.0_spmd.clone.sunk | while | flops 113377280 | bytes 832115 | solution.py:51
  97.3 3.9 convolution_add_fusion.2
  101.2 3.9 convolution_add_fusion.2
  105.1 3.8 convolution_add_fusion.2
  109.0 3.8 convolution_add_fusion.2
  112.8 3.8 convolution_add_fusion.2
  116.7 3.8 convolution_add_fusion.2
  120.6 3.8 convolution_add_fusion.2
  124.5 3.8 convolution_add_fusion.2
  128.4 3.8 convolution_add_fusion.2
  132.3 3.8 convolution_add_fusion.2
  140.1 3.8 convolution_add_fusion.2
  147.9 3.8 convolution_add_fusion.2
  155.6 3.8 convolution_add_fusion.2
  161.2 24.1 %all-gather = bf16[16,64,32]{1,2,0:T(8,128)(2,1)S(1)} all-gather(bf16[1,64,32]{1,2,0:T(8,128)(2,1)S(1)} %fusion.34), channel_id=1, replica_groups=mesh['row'=16,'col'=16] {'col'}, dimensions={0}, use_global_device_ids=true | all-gather | bytes 69632 | tf_op jit(solution)/shard_map/all_gather | solution.py:74
  185.7 46.0 %reduce-scatter.5.cloned.1.call-done = f32[16,256]{1,0:T(8,128)} async-done(((f32[16,4096]{1,0:T(8,128)}), f32[16,256]{1,0:T(8,128)}) %reduce-scatter.5.cloned.1.call-update) | async-done | bytes 16400 | tf_op jit(solution)/shard_map/reduce_scatter | solution.py:92
  232.6 73.9 %all-reduce = (f32[16]{0:T(128)S(1)}, f32[16]{0:T(128)S(1)}) all-reduce(f32[16]{0:T(128)S(1)} %multiply_reduce_fusion.5, f32[16]{0:T(128)S(1)} %multiply_reduce_fusion.4), channel_id=1, replica_groups=mesh['row'=16,'col'=16] {'row','col'}, use_global_device_ids=true, to_apply=%region_1.0 | all-reduce | flops 32 | bytes 256 | tf_op jit(solution)/shard_map/psum | solution.py:71
  307.4 74.3 %psum.23 = f32[16]{0:T(128)S(1)} all-reduce(f32[16]{0:T(128)S(1)} %get-tuple-element.228), channel_id=1, replica_groups=mesh['row'=16,'col'=16] {'row','col'}, use_global_device_ids=true, to_apply=%region_10.11 | all-reduce | flops 16 | bytes 128 | tf_op jit(solution)/shard_map/psum | solution.py:98
  381.7 30.4 %all_gather.18 = bf16[16,4096]{1,0:T(8,128)(2,1)S(1)} all-gather(bf16[16,256]{1,0:T(8,128)(2,1)S(1)} %get-tuple-element.230), channel_id=1, replica_groups=mesh['row'=16,'col'=16] {'row'}, dimensions={1}, use_global_device_ids=true | all-gather | bytes 139264 | tf_op jit(solution)/shard_map/all_gather | solution.py:110
  412.1 15.4 %while.23 = (s32[]{:T(128)}, f32[16,1024]{1,0:T(8,128)S(1)}, bf16[4,16,1024]{2,1,0:T(8,128)(2,1)S(1)}, f32[]{:T(128)}, f32[1024]{0:T(1024)S(1)}, /*index=5*/f32[...) while((s32[]{:T(128)}, f32[16,1024]{1,0:T(8,128)S(1)}, ...), condition=%wide.region_13.14_spmd.clone, body=%wide.region_12.13_spmd.clone.sunk | while | flops 113278976 | bytes 312947 | solution.py:51
  429.2 71.2 %reduce-scatter.7.cloned.1.call-done = f32[64,16]{1,0:T(8,128)} async-done(((f32[1024,16]{1,0:T(8,128)}), f32[64,16]{1,0:T(8,128)}) %reduce-scatter.7.cloned.1.call-update) | async-done | bytes 4112
  (76 shorter events, 34.9 us)
Async XLA Ops:
  7.2 224.5 %reduce-scatter.5.cloned.1.call-start = ((), (), s32[]{:S(2)}) async-start(), calls=%async_computation.2 | async-start | bytes 278528 | tf_op jit(solution)/shard_map/reduce_scatter | solution.py:92
  66.3 0.7 copy-start.1
  159.5 0.7 copy-start
  159.5 1.6 copy-start.5
  159.5 1.6 copy-start.7
  160.2 340.2 %reduce-scatter.7.cloned.1.call-start = ((), (), s32[]{:S(2)}) async-start(), calls=%async_computation.3 | async-start | bytes 557056
  160.3 25.2 %copy-start.3 = (f32[16,256]{1,0:T(8,128)S(1)}, f32[16,256]{1,0:T(8,128)}, u32[]{:S(2)}) copy-start(f32[16,256]{1,0:T(8,128)} %param.20) | copy-start | bytes 49156
  185.3 121.3 %copy-start.6 = (f32[16,256]{1,0:T(8,128)S(1)}, f32[16,256]{1,0:T(8,128)}, u32[]{:S(2)}) copy-start(f32[16,256]{1,0:T(8,128)} %param.19) | copy-start | bytes 49156
  231.7 74.9 %copy-start.4 = (f32[16,256]{1,0:T(8,128)S(1)}, f32[16,256]{1,0:T(8,128)}, u32[]{:S(2)}) copy-start(f32[16,256]{1,0:T(8,128)} %reduce-scatter.5.cloned.1.call-done) | copy-start | bytes 49156
  307.4 121.2 %copy-start.2 = (f32[16,256]{1,0:T(8,128)}, f32[16,256]{1,0:T(8,128)S(1)}, u32[]{:S(2)}) copy-start(f32[16,256]{1,0:T(8,128)S(1)} %get-tuple-element.229) | copy-start | bytes 49156
  427.5 73.7 %copy-start.8 = (f32[64]{0:T(128)S(1)}, f32[64]{0:T(128)}, u32[]{:S(2)}) copy-start(f32[64]{0:T(128)} %param.18) | copy-start | bytes 772
Sparse Core Ops, SparseCore 0:
  160.3 71.2 reduce-scatter.4
  428.7 71.7 reduce-scatter.6
where the time goes:
time: 509 us
  blocking collectives  291 us (57%)
  waiting for transfers between devices  117 us (23%)
  matrix products  76.8 us (15%)
  between operations  14.9 us (3%)
    dot_general x20, matrix products, one_block(): lax.dot_general(vec_blk, kern_vals, contract_last, preferred_element_type...  76.8 us
    psum x1, blocking collectives, per_device(): lax.psum(jnp.sum(residual_new * residual_new, axis=1), ('row', 'col'))  74.3 us
    psum x1, blocking collectives, per_device(): norm_now = lax.psum(jnp.sum(residual * residual, axis=1), ('row', 'col'))  73.9 us
    unnamed x3, waiting for transfers between devices  71.2 us
    reduce_scatter x1, waiting for transfers between devices, per_device(): lax.psum_scatter(partial_rows, 'col', scatter_dimension=1, tiled=True)  46 us
    all_gather x1, blocking collectives, per_device(): col_pts = lax.all_gather(scaled, 'row', axis=1, tiled=True)  37.8 us
    all_gather x1, blocking collectives, per_device(): lax.all_gather(w_low, 'row', axis=1, tiled=True)  30.4 us
    all_gather x1, blocking collectives, per_device(): lax.all_gather(dir_low, 'row', axis=1, tiled=True)  30.2 us
  transfers between devices with their start and end apart: 2, of which 2 were waited for; matrix products, arithmetic and copies ran while one was open for 0% of the time, Pallas kernels for 0%

commit v1 on v0

--- a/solution.py
+++ b/solution.py
@@ -1,3 +1,4 @@
+import functools
 import math
 import jax
 import jax.numpy as jnp
@@ -7,6 +8,19 @@
 root_five = math.sqrt(5.0)
 contract_first = (((0,), (0,)), ((), ()))
 contract_last = (((1,), (1,)), ((), ()))
+
+
+def copies_pack(target, lane_axis):
+    g_now = jnp.concatenate(
+        lax.all_to_all(
+            jnp.stack([target for _ in range(lax.axis_size(lane_axis))], 0), lane_axis, 0, 0
+        ),
+        1,
+    )
+    return g_now
+
+
+_take_slices = functools.partial(copies_pack, lane_axis="row")
 
 
 def square_norms(scaled):
@@ -81,13 +95,7 @@
     pts_piece = col_pts
     sq_piece = col_sq
     partial_rows = kernel_apply(
-        start_rows,
-        row_pts,
-        row_sq,
-        pts_piece,
-        sq_piece,
-        lax.all_gather(dir_low, "row", axis=1, tiled=True),
-        signal_scalar,
+        start_rows, row_pts, row_sq, pts_piece, sq_piece, _take_slices(dir_low), signal_scalar
     )
     kernel_out = lax.psum_scatter(partial_rows, "col", scatter_dimension=1, tiled=True)
     image_vec = kernel_out + noise_var[0] * direction

time: 509 us -> 488 us (0.959)
  blocking collectives: 291 us -> 258 us
  starting transfers between devices: 0.08 us -> 9.66 us
    all_gather x1 -> x0, blocking collectives: 30.2 us -> none  [per_device(): lax.all_gather(dir_low, 'row', axis=1, tiled=True)]
    all_to_all x0 -> x1, starting transfers between devices: none -> 9.58 us  [copies_pack(): lax.all_to_all(jnp.stack([target for _ in range(lax.axis_size(lane_axis))...]
  transfers between devices with their start and end apart: 2 -> 3, of which waited for: 2 -> 2; matrix products, arithmetic and copies ran while one was open for 0% -> 0% of each run, Pallas kernels for 0% -> 0%
where the time goes in v1:
time: 488 us; the launch traced here: 487 us
  blocking collectives  258 us (53%)
  waiting for transfers between devices  118 us (24%)
  matrix products  76.8 us (16%)
  between operations  14.9 us (3%)
  starting transfers between devices  9.66 us (2%)
  other arithmetic  4.93 us (1%)
    dot_general x20, matrix products, one_block(): lax.dot_general(vec_blk, kern_vals, contract_last, preferred_element_type...  76.8 us
    psum x1, blocking collectives, per_device(): lax.psum(jnp.sum(residual_new * residual_new, axis=1), ('row', 'col'))  74.3 us
    psum x1, blocking collectives, per_device(): norm_now = lax.psum(jnp.sum(residual * residual, axis=1), ('row', 'col'))  74 us
    unnamed x3, waiting for transfers between devices  71.2 us
    reduce_scatter x1, waiting for transfers between devices, per_device(): lax.psum_scatter(partial_rows, 'col', scatter_dimension=1, tiled=True)  46.8 us
    all_gather x1, blocking collectives, per_device(): col_pts = lax.all_gather(scaled, 'row', axis=1, tiled=True)  34.9 us
    all_gather x1, blocking collectives, per_device(): lax.all_gather(w_low, 'row', axis=1, tiled=True)  30.4 us
    all_gather x1, blocking collectives, per_device(): lax.all_gather(cand_scaled, 'col', axis=1, tiled=True)  24.1 us
  transfers between devices with their start and end apart: 3, of which 2 were waited for; matrix products, arithmetic and copies ran while one was open for 0% of the time, Pallas kernels for 0%

profile of v1, /device:TPU:2, one launch (start us, length us, event | category | flops | bytes accessed | tf_op | source)
XLA Modules:
  0.0 486.8 jit_solution(6930115395424392446)
XLA Ops:
  8.5 9.6 %all-to-all-start = ((bf16[16,16,256]{2,1,0:T(8,128)(2,1)}), bf16[16,16,256]{2,1,0:T(8,128)(2,1)S(1)}, u32[]{:S(2)}, u32[]{:S(2)}) async-start(bf16[16,16,256]{2,1,0:T(8,128)(2,1)} %stack.2), calls=%async_computation | async-start | bytes 262144 | tf_op jit(solution)/shard_map/all_to_all | solution.py:15
  19.0 34.9 %all_gather.13 = bf16[32,4096]{1,0:T(8,128)(2,1)S(1)} all-gather(bf16[32,256]{1,0:T(8,128)(2,1)S(1)} %divide_convert_fusion), channel_id=1, replica_groups=mesh['row'=16,'col'=16] {'row'}, dimensions={1}, use_global_device_ids=true | all-gather | bytes 278528 | tf_op jit(solution)/shard_map/all_gather | solution.py:90
  54.9 20.5 %all_gather.12 = bf16[32,4096]{1,0:T(8,128)(2,1)S(1)} all-gather(bf16[32,256]{1,0:T(8,128)(2,1)S(1)} %divide_convert_fusion), channel_id=1, replica_groups=mesh['row'=16,'col'=16] {'col'}, dimensions={1}, use_global_device_ids=true | all-gather | bytes 278528 | tf_op jit(solution)/shard_map/all_gather | solution.py:87
  75.5 62.2 %while.22 = (s32[]{:T(128)}, f32[16,4096]{1,0:T(8,128)S(1)}, bf16[16,16,256]{2,1,0:T(8,128)(2,1)S(1)}, f32[]{:T(128)}, f32[4096]{0:T(1024)S(1)}, /*index=5*/f32[...) while((s32[]{:T(128)}, f32[16,4096]{1,0:T(8,128)S(1)}, ...), condition=%wide.region_5.6_spmd.clone, body=%wide.region_4.0_spmd.clone.sunk | while | flops 113377280 | bytes 832115 | solution.py:65
  79.4 3.8 convolution_add_fusion.2
  83.3 3.8 convolution_add_fusion.2
  87.2 3.8 convolution_add_fusion.2
  91.1 3.8 convolution_add_fusion.2
  95.0 3.8 convolution_add_fusion.2
  98.9 3.8 convolution_add_fusion.2
  102.8 3.8 convolution_add_fusion.2
  106.6 3.8 convolution_add_fusion.2
  110.5 3.8 convolution_add_fusion.2
  114.4 3.8 convolution_add_fusion.2
  118.3 3.8 convolution_add_fusion.2
  126.1 3.8 convolution_add_fusion.2
  133.8 3.8 convolution_add_fusion.2
  138.6 24.1 %all-gather = bf16[16,64,32]{1,2,0:T(8,128)(2,1)S(1)} all-gather(bf16[1,64,32]{1,2,0:T(8,128)(2,1)S(1)} %fusion.34), channel_id=1, replica_groups=mesh['row'=16,'col'=16] {'col'}, dimensions={0}, use_global_device_ids=true | all-gather | bytes 69632 | tf_op jit(solution)/shard_map/all_gather | solution.py:88
  163.0 46.8 %reduce-scatter.5.cloned.1.call-done = f32[16,256]{1,0:T(8,128)} async-done(((f32[16,4096]{1,0:T(8,128)}), f32[16,256]{1,0:T(8,128)}) %reduce-scatter.5.cloned.1.call-update) | async-done | bytes 16400 | tf_op jit(solution)/shard_map/reduce_scatter | solution.py:100
  210.8 74.0 %all-reduce = (f32[16]{0:T(128)S(1)}, f32[16]{0:T(128)S(1)}) all-reduce(f32[16]{0:T(128)S(1)} %multiply_reduce_fusion.5, f32[16]{0:T(128)S(1)} %multiply_reduce_fusion.4), channel_id=1, replica_groups=mesh['row'=16,'col'=16] {'row','col'}, use_global_device_ids=true, to_apply=%region_1.0 | all-reduce | flops 32 | bytes 256 | tf_op jit(solution)/shard_map/psum | solution.py:85
  285.5 74.3 %psum.23 = f32[16]{0:T(128)S(1)} all-reduce(f32[16]{0:T(128)S(1)} %get-tuple-element.204), channel_id=1, replica_groups=mesh['row'=16,'col'=16] {'row','col'}, use_global_device_ids=true, to_apply=%region_10.11 | all-reduce | flops 16 | bytes 128 | tf_op jit(solution)/shard_map/psum | solution.py:106
  359.9 30.4 %all_gather.14 = bf16[16,4096]{1,0:T(8,128)(2,1)S(1)} all-gather(bf16[16,256]{1,0:T(8,128)(2,1)S(1)} %get-tuple-element.206), channel_id=1, replica_groups=mesh['row'=16,'col'=16] {'row'}, dimensions={1}, use_global_device_ids=true | all-gather | bytes 139264 | tf_op jit(solution)/shard_map/all_gather | solution.py:118
  390.2 15.4 %while.23 = (s32[]{:T(128)}, f32[16,1024]{1,0:T(8,128)S(1)}, bf16[4,16,1024]{2,1,0:T(8,128)(2,1)S(1)}, f32[]{:T(128)}, f32[1024]{0:T(1024)S(1)}, /*index=5*/f32[...) while((s32[]{:T(128)}, f32[16,1024]{1,0:T(8,128)S(1)}, ...), condition=%wide.region_13.14_spmd.clone, body=%wide.region_12.13_spmd.clone.sunk | while | flops 113278976 | bytes 312947 | solution.py:65
  407.4 71.2 %reduce-scatter.7.cloned.1.call-done = f32[64,16]{1,0:T(8,128)} async-done(((f32[1024,16]{1,0:T(8,128)}), f32[64,16]{1,0:T(8,128)}) %reduce-scatter.7.cloned.1.call-update) | async-done | bytes 4112
  (76 shorter events, 35.7 us)
Async XLA Ops:
  8.5 67.0 %all-to-all-start = ((bf16[16,16,256]{2,1,0:T(8,128)(2,1)}), bf16[16,16,256]{2,1,0:T(8,128)(2,1)S(1)}, u32[]{:S(2)}, u32[]{:S(2)}) async-start(bf16[16,16,256]{2,1,0:T(8,128)(2,1)} %stack.2), calls=%async_computation | async-start | bytes 262144 | tf_op jit(solution)/shard_map/all_to_all | solution.py:15
  18.1 191.6 %reduce-scatter.5.cloned.1.call-start = ((), (), s32[]{:S(2)}) async-start(), calls=%async_computation.3 | async-start | bytes 278528 | tf_op jit(solution)/shard_map/reduce_scatter | solution.py:100
  75.5 63.0 %copy-start.5 = (f32[32,64]{1,0:T(8,128)S(1)}, f32[32,64]{1,0:T(8,128)}, u32[]{:S(2)}) copy-start(f32[32,64]{1,0:T(8,128)} %param.14) | copy-start | bytes 24580
  75.5 63.0 %copy-start.7 = (f32[32]{0:T(128)S(1)}, f32[32]{0:T(128)}, u32[]{:S(2)}) copy-start(f32[32]{0:T(128)} %param.15) | copy-start | bytes 388
  137.7 0.7 copy-start
  137.7 25.1 %copy-start.3 = (f32[16,256]{1,0:T(8,128)S(1)}, f32[16,256]{1,0:T(8,128)}, u32[]{:S(2)}) copy-start(f32[16,256]{1,0:T(8,128)} %param.20) | copy-start | bytes 49156
  137.7 72.0 %copy-start.1 = (f32[16,256]{1,0:T(8,128)S(1)}, f32[16,256]{1,0:T(8,128)}, u32[]{:S(2)}) copy-start(f32[16,256]{1,0:T(8,128)} %param.21) | copy-start | bytes 49156
  138.4 340.1 %reduce-scatter.7.cloned.1.call-start = ((), (), s32[]{:S(2)}) async-start(), calls=%async_computation.4 | async-start | bytes 557056
  162.6 122.1 %copy-start.6 = (f32[16,256]{1,0:T(8,128)S(1)}, f32[16,256]{1,0:T(8,128)}, u32[]{:S(2)}) copy-start(f32[16,256]{1,0:T(8,128)} %param.19) | copy-start | bytes 49156
  209.8 75.0 %copy-start.4 = (f32[16,256]{1,0:T(8,128)S(1)}, f32[16,256]{1,0:T(8,128)}, u32[]{:S(2)}) copy-start(f32[16,256]{1,0:T(8,128)} %reduce-scatter.5.cloned.1.call-done) | copy-start | bytes 49156
  285.5 121.2 %copy-start.2 = (f32[16,256]{1,0:T(8,128)}, f32[16,256]{1,0:T(8,128)S(1)}, u32[]{:S(2)}) copy-start(f32[16,256]{1,0:T(8,128)S(1)} %get-tuple-element.205) | copy-start | bytes 49156
  405.7 73.7 %copy-start.8 = (f32[64]{0:T(128)S(1)}, f32[64]{0:T(128)}, u32[]{:S(2)}) copy-start(f32[64]{0:T(128)} %param.18) | copy-start | bytes 772
Sparse Core Ops, SparseCore 0:
  138.5 71.1 reduce-scatter.4
  406.8 71.7 reduce-scatter.6
